TPU v7x, 512 devices: a whole 4x8x8 slice. The times are simulated.
512 devices in a mesh: expert: 64 (over y, z_hi, core), narrow: 8 (over z_lo, x).
Axes of the slice: x: 4, y: 8, z: 8 (z_hi: 4, z_lo: 2; z = z_hi * 2 + z_lo), core: 2. Of those that a mesh axis runs over, the one named last changes fastest.
Arguments:
- tokens: bfloat16 [3072, 4096], P('expert', 'narrow'), may hold values from -6 to 6
- route_ids: int32 [3072, 8], P('expert'), may hold values from 0 to 63, all different within a row; in each aligned block of 48 rows (0 to 47, 48 to 95, ...) at most 12 rows name the same one
- route_weight: bfloat16 [3072, 8], P('expert'), may hold values from 0.049804688 to 0.5
- partner: int32 [64], replicated, may hold values from 0 to 63, as said below
- old_place: int32 [64], replicated, may hold values from 0 to 63, each once
- gate_weight: bfloat16 [64, 768, 4096], P('expert', 'narrow'), may hold values from -0.09375 to 0.09375
- up_weight: bfloat16 [64, 768, 4096], P('expert', 'narrow'), may hold values from -0.09375 to 0.09375
- down_weight: bfloat16 [64, 768, 4096], P('expert', None, 'narrow'), may hold values from -0.21875 to 0.21875
Outputs:
- layer_out: bfloat16 [3072, 4096], P('expert', 'narrow')
- new_gate: bfloat16 [64, 768, 4096], P('expert', 'narrow')
- new_up: bfloat16 [64, 768, 4096], P('expert', 'narrow')
- new_down: bfloat16 [64, 768, 4096], P('expert', None, 'narrow')
Inputs may be any that keep to these rules, and one draw needn't show every extreme that they name: partner[partner[s]] == s for every slot; slots with partner[s] == s keep their weights; the number of pairs varies between draws from 1 to 32. `old_place`: a permutation of the experts. `route_ids`: each row names 8 different experts; among the 48 tokens of one index of expert, no expert is named by more than 12 tokens.
All inputs are finite; a program needn't handle non-finite values.
Results may differ from a plain program's by a relative error of at most 0.0058.
Values may be sent and summed in bfloat16 or wider, within the bound.
No kernel may reach another device: no remote copies, remote signals or barrier semaphores. Data moves between devices by JAX's collectives and lax.ppermute only.
A program may use at most 128 MiB of HBM per device.

v0:
```python
import jax
import jax.numpy as jnp
from jax import lax
from jax.sharding import PartitionSpec as P


def slot_layout(route_ids, route_weight, holder, groups):
    tokens_here, top_count = route_ids.shape
    capacity = 2 * tokens_here * top_count // groups
    slot_ids = jnp.arange(groups, dtype=jnp.int32)
    matches = (holder[None, None, :] == route_ids[:, :, None]).astype(jnp.int32)
    target = jnp.sum(matches * slot_ids[None, None, :], axis=2)
    onehot = matches.reshape(tokens_here * top_count, groups)
    running = jnp.cumsum(onehot, axis=0) - 1
    position = jnp.sum(onehot * running, axis=1).reshape(tokens_here, top_count)
    row_index = target * capacity + position
    buffer_rows = jnp.arange(groups * capacity, dtype=jnp.int32)
    row_hits = buffer_rows[:, None, None] == row_index[None, :, :]
    dispatch = jnp.sum(row_hits.astype(jnp.float32), axis=2).astype(jnp.bfloat16)
    token_hits = row_index[:, :, None] == buffer_rows[None, None, :]
    combine = jnp.sum(
        jnp.where(token_hits, route_weight[:, :, None], jnp.zeros((), jnp.bfloat16)), axis=1
    )
    return (dispatch, combine, capacity)


def contract_last(left, right):
    return lax.dot_general(
        left, right, (((1,), (1,)), ((), ())), preferred_element_type=jnp.float32
    )


def body(tokens, route_ids, route_weight, partner, old_place, gate_weight, up_weight, down_weight):
    groups = lax.axis_size("expert")
    gate_flat = gate_weight.reshape(groups, -1)
    up_flat = up_weight.reshape(groups, -1)
    down_flat = down_weight.reshape(groups, -1)
    spread = (
        lax.all_to_all(gate_flat, "expert", split_axis=0, concat_axis=0, tiled=True),
        lax.all_to_all(up_flat, "expert", split_axis=0, concat_axis=0, tiled=True),
        lax.all_to_all(down_flat, "expert", split_axis=0, concat_axis=0, tiled=True),
    )
    gate_order = jnp.take(spread[0], partner, axis=0)
    up_order = jnp.take(spread[1], partner, axis=0)
    down_order = jnp.take(spread[2], partner, axis=0)
    arrived = (
        lax.all_to_all(gate_order, "expert", split_axis=0, concat_axis=0, tiled=True),
        lax.all_to_all(up_order, "expert", split_axis=0, concat_axis=0, tiled=True),
        lax.all_to_all(down_order, "expert", split_axis=0, concat_axis=0, tiled=True),
    )
    new_gate = arrived[0].reshape(gate_weight.shape)
    new_up = arrived[1].reshape(up_weight.shape)
    new_down = arrived[2].reshape(down_weight.shape)
    holder = jnp.take(old_place, partner)
    gate_block = new_gate[0]
    up_block = new_up[0]
    down_block = new_down[0]
    dispatch, combine, capacity = slot_layout(route_ids, route_weight, holder, groups)
    full_tokens = lax.all_gather(tokens, "narrow", axis=1, tiled=True)
    outgoing = jnp.dot(dispatch, full_tokens, preferred_element_type=jnp.float32).astype(
        jnp.bfloat16
    )
    arrived_rows = lax.all_to_all(
        outgoing.reshape(groups, capacity, -1), "expert", split_axis=0, concat_axis=0, tiled=True
    )
    flat_rows = arrived_rows.reshape(-1, arrived_rows.shape[2])
    gate_sum = contract_last(flat_rows, gate_block)
    up_sum = contract_last(flat_rows, up_block)
    hidden = (jax.nn.silu(gate_sum) * up_sum).astype(jnp.bfloat16)
    produced = (
        jnp.dot(
            lax.all_gather(hidden, "narrow", axis=1, tiled=True),
            down_block,
            preferred_element_type=jnp.float32,
        )
        .astype(jnp.bfloat16)
        .reshape(arrived_rows.shape[0], arrived_rows.shape[1], -1)
    )
    returned = lax.all_to_all(produced, "expert", split_axis=0, concat_axis=0, tiled=True)
    layer_out = jnp.dot(
        combine, returned.reshape(-1, returned.shape[2]), preferred_element_type=jnp.float32
    ).astype(jnp.bfloat16)
    return (layer_out, new_gate, new_up, new_down)


def solution(mesh):
    return jax.shard_map(
        body,
        mesh=mesh,
        in_specs=(
            P("expert", "narrow"),
            P("expert", None),
            P("expert", None),
            P(),
            P(),
            P("expert", "narrow", None),
            P("expert", "narrow", None),
            P("expert", None, "narrow"),
        ),
        out_specs=(
            P("expert", "narrow"),
            P("expert", "narrow", None),
            P("expert", "narrow", None),
            P("expert", None, "narrow"),
        ),
        check_vma=False,
    )
```

profile of v0, /device:TPU:80, one launch (start us, length us, event | category | flops | bytes accessed | tf_op | source)
XLA Modules:
  0.0 634.3 jit_solution(16042910142443403601)
XLA Ops:
  12.4 5.5 reduce.9
  19.4 16.0 %all-to-all-start.5 = ((bf16[64,2,3072]{2,1,0:T(2,128)(2,1)}), bf16[64,2,3072]{2,1,0:T(2,128)(2,1)S(1)}, u32[]{:S(2)}, u32[]{:S(2)}) async-start(bf16[64,2,3072]{2,1,0:T(2,128)(2,1)} %reshape.175), calls=%async_computation.5 | async-start | bytes 1572864 | tf_op jit(solution)/shard_map/all_to_all | solution.py:41
  36.7 5.5 reduce.10
  43.6 17.1 %all-to-all-done.5 = bf16[64,2,3072]{2,1,0:T(2,128)(2,1)S(1)} async-done(((bf16[64,2,3072]{2,1,0:T(2,128)(2,1)}), bf16[64,2,3072]{2,1,0:T(2,128)(2,1)S(1)}, u32[]{:S(2)}, u32[]{:S(2)}) %all-to-all-start.5) | async-done | bytes 786464 | tf_op jit(solution)/shard_map/all_to_all | solution.py:41
  60.7 6.1 all-to-all-start.1
  68.1 5.5 reduce.11
  75.1 16.9 %all-to-all-done.1 = bf16[64,2,3072]{2,1,0:T(2,128)(2,1)} async-done(((bf16[64,2,3072]{2,1,0:T(2,128)(2,1)}), bf16[64,2,3072]{2,1,0:T(2,128)(2,1)}, u32[]{:S(2)}, u32[]{:S(2)}) %all-to-all-start.1) | async-done | bytes 786464 | tf_op jit(solution)/shard_map/all_to_all | solution.py:39
  92.0 6.3 all-to-all-start.3
  101.3 4.9 reshape.172
  108.6 15.0 %all-to-all-done.3 = bf16[64,2,3072]{2,1,0:T(2,128)(2,1)} async-done(((bf16[64,2,3072]{2,1,0:T(2,128)(2,1)}), bf16[64,2,3072]{2,1,0:T(2,128)(2,1)}, u32[]{:S(2)}, u32[]{:S(2)}) %all-to-all-start.3) | async-done | bytes 786464 | tf_op jit(solution)/shard_map/all_to_all | solution.py:40
  135.2 5.5 all-to-all-start.4
  143.4 22.8 %all-to-all-done.4 = bf16[64,2,3072]{2,1,0:T(2,128)(2,1)S(1)} async-done(((bf16[64,2,3072]{2,1,0:T(2,128)(2,1)}), bf16[64,2,3072]{2,1,0:T(2,128)(2,1)S(1)}, u32[]{:S(2)}, u32[]{:S(2)}) %all-to-all-start.4) | async-done | bytes 786464 | tf_op jit(solution)/shard_map/all_to_all | solution.py:48
  166.3 5.5 all-to-all-start.2
  175.0 37.4 %all_gather.6 = bf16[48,4096]{1,0:T(8,128)(2,1)S(1)} all-gather(bf16[48,512]{1,0:T(8,128)(2,1)S(1)} %copy-done.10), channel_id=1, replica_groups=mesh['expert'=64,'narrow'=8] {'narrow'}, dimensions={1}, use_global_device_ids=true | all-gather | bytes 442368 | tf_op jit(solution)/shard_map/all_gather | solution.py:59
  216.8 9.7 %reshape.111 = bf16[64,12,4096]{2,1,0:T(8,128)(2,1)} reshape(bf16[768,4096]{1,0:T(8,128)(2,1)} %convolution_convert_fusion) | data formatting | bytes 12582912 | tf_op jit(solution)/shard_map/reshape | solution.py:64
  227.4 15.7 %all-to-all-start = ((bf16[64,12,4096]{2,1,0:T(8,128)(2,1)}), bf16[64,12,4096]{2,1,0:T(8,128)(2,1)}, u32[]{:S(2)}, u32[]{:S(2)}) async-start(bf16[64,12,4096]{2,1,0:T(8,128)(2,1)} %reshape.111), calls=%async_computation | async-start | bytes 16777216 | tf_op jit(solution)/shard_map/all_to_all | solution.py:63
  256.3 206.2 %all-to-all-done = bf16[64,12,4096]{2,1,0:T(8,128)(2,1)} async-done(((bf16[64,12,4096]{2,1,0:T(8,128)(2,1)}), bf16[64,12,4096]{2,1,0:T(8,128)(2,1)}, u32[]{:S(2)}, u32[]{:S(2)}) %all-to-all-start) | async-done | bytes 6291488 | tf_op jit(solution)/shard_map/all_to_all | solution.py:63
  462.5 10.0 %reshape.112 = bf16[768,4096]{1,0:T(8,128)(2,1)} reshape(bf16[64,12,4096]{2,1,0:T(8,128)(2,1)} %all-to-all-done) | data formatting | bytes 12582912 | tf_op jit(solution)/shard_map/reshape | solution.py:66
  472.5 5.0 fusion.6
  482.1 54.6 %all_to_all.76 = bf16[64,2,3072]{2,1,0:T(2,128)(2,1)S(1)} all-to-all(bf16[64,2,3072]{2,1,0:T(2,128)(2,1)S(1)} %reshape.177), channel_id=1, replica_groups=mesh['expert'=64,'narrow'=8] {'expert'}, dimensions={0} | all-to-all | bytes 1572864 | tf_op jit(solution)/shard_map/all_to_all | solution.py:49
  538.7 5.8 reduce.4
  546.4 29.8 %all-gather.2.cloned.1.call-done = bf16[768,768]{0,1:T(8,128)(2,1)} async-done(((bf16[768,96]{0,1:T(8,128)(2,1)}), bf16[768,768]{0,1:T(8,128)(2,1)}) %all-gather.2.cloned.1.call-update) | async-done | bytes 1179664 | tf_op jit(solution)/shard_map/all_gather | solution.py:72
  579.7 15.6 %all-to-all-start.7 = ((bf16[64,12,512]{2,1,0:T(8,128)(2,1)}), bf16[64,12,512]{2,1,0:T(8,128)(2,1)S(1)}, u32[]{:S(2)}, u32[]{:S(2)}) async-start(bf16[64,12,512]{2,1,0:T(8,128)(2,1)} %reshape.113), calls=%async_computation.7 | async-start | bytes 2097152 | tf_op jit(solution)/shard_map/all_to_all | solution.py:79
  600.6 25.5 %all-to-all-done.7 = bf16[64,12,512]{2,1,0:T(8,128)(2,1)S(1)} async-done(((bf16[64,12,512]{2,1,0:T(8,128)(2,1)}), bf16[64,12,512]{2,1,0:T(8,128)(2,1)S(1)}, u32[]{:S(2)}, u32[]{:S(2)}) %all-to-all-start.7) | async-done | bytes 786464 | tf_op jit(solution)/shard_map/all_to_all | solution.py:79
  (88 shorter events, 71.5 us)
Async XLA Ops:
  7.2 91.2 %copy-start = (s32[64]{0:T(128)S(1)}, s32[64]{0:T(128)}, u32[]{:S(2)}) copy-start(s32[64]{0:T(128)} %param.14) | copy-start | bytes 772
  19.4 16.0 %copy-start.8 = (bf16[1,96,4096]{2,1,0:T(8,128)(2,1)S(1)}, bf16[1,96,4096]{2,1,0:T(8,128)(2,1)}, u32[]{:S(2)}) copy-start(bf16[1,96,4096]{2,1,0:T(8,128)(2,1)} %param.15) | copy-start | bytes 2359300
  19.4 41.3 %all-to-all-start.5 = ((bf16[64,2,3072]{2,1,0:T(2,128)(2,1)}), bf16[64,2,3072]{2,1,0:T(2,128)(2,1)S(1)}, u32[]{:S(2)}, u32[]{:S(2)}) async-start(bf16[64,2,3072]{2,1,0:T(2,128)(2,1)} %reshape.175), calls=%async_computation.5 | async-start | bytes 1572864 | tf_op jit(solution)/shard_map/all_to_all | solution.py:41
  43.6 23.2 %copy-start.9 = (bf16[1,96,4096]{2,1,0:T(8,128)(2,1)S(1)}, bf16[1,96,4096]{2,1,0:T(8,128)(2,1)}, u32[]{:S(2)}) copy-start(bf16[1,96,4096]{2,1,0:T(8,128)(2,1)} %param.16) | copy-start | bytes 2359300
  60.7 31.3 %all-to-all-start.1 = ((bf16[64,2,3072]{2,1,0:T(2,128)(2,1)}), bf16[64,2,3072]{2,1,0:T(2,128)(2,1)}, u32[]{:S(2)}, u32[]{:S(2)}) async-start(bf16[64,2,3072]{2,1,0:T(2,128)(2,1)} %reshape.171), calls=%async_computation.1 | async-start | bytes 1572864 | tf_op jit(solution)/shard_map/all_to_all | solution.py:39
  73.6 24.7 %copy-start.13 = (s32[64]{0:T(128)S(1)}, s32[64]{0:T(128)}, u32[]{:S(2)}) copy-start(s32[64]{0:T(128)} %param.13) | copy-start | bytes 772
  92.0 31.5 %all-to-all-start.3 = ((bf16[64,2,3072]{2,1,0:T(2,128)(2,1)}), bf16[64,2,3072]{2,1,0:T(2,128)(2,1)}, u32[]{:S(2)}, u32[]{:S(2)}) async-start(bf16[64,2,3072]{2,1,0:T(2,128)(2,1)} %reshape.167), calls=%async_computation.3 | async-start | bytes 1572864 | tf_op jit(solution)/shard_map/all_to_all | solution.py:40
  128.9 1.1 copy-start.3
  135.2 31.0 %all-to-all-start.4 = ((bf16[64,2,3072]{2,1,0:T(2,128)(2,1)}), bf16[64,2,3072]{2,1,0:T(2,128)(2,1)S(1)}, u32[]{:S(2)}, u32[]{:S(2)}) async-start(bf16[64,2,3072]{2,1,0:T(2,128)(2,1)} %reshape.169), calls=%async_computation.4 | async-start | bytes 1572864 | tf_op jit(solution)/shard_map/all_to_all | solution.py:48
  142.0 29.8 %copy-start.11 = (s32[48,8]{0,1:T(8,128)S(1)}, s32[48,8]{0,1:T(8,128)}, u32[]{:S(2)}) copy-start(s32[48,8]{0,1:T(8,128)} %param.11) | copy-start | bytes 4612
  143.4 31.5 %copy-start.10 = (bf16[48,512]{1,0:T(8,128)(2,1)S(1)}, bf16[48,512]{1,0:T(8,128)(2,1)}, u32[]{:S(2)}) copy-start(bf16[48,512]{1,0:T(8,128)(2,1)} %param.10) | copy-start | bytes 147460
  166.3 60.3 %all-to-all-start.2 = ((bf16[64,2,3072]{2,1,0:T(2,128)(2,1)}), bf16[64,2,3072]{2,1,0:T(2,128)(2,1)S(1)}, u32[]{:S(2)}, u32[]{:S(2)}) async-start(bf16[64,2,3072]{2,1,0:T(2,128)(2,1)} %reshape.173), calls=%async_computation.2 | async-start | bytes 1572864 | tf_op jit(solution)/shard_map/all_to_all | solution.py:47
  226.6 0.9 copy-start.5
  227.4 235.0 %all-to-all-start = ((bf16[64,12,4096]{2,1,0:T(8,128)(2,1)}), bf16[64,12,4096]{2,1,0:T(8,128)(2,1)}, u32[]{:S(2)}, u32[]{:S(2)}) async-start(bf16[64,12,4096]{2,1,0:T(8,128)(2,1)} %reshape.111), calls=%async_computation | async-start | bytes 16777216 | tf_op jit(solution)/shard_map/all_to_all | solution.py:63
  243.1 333.1 %all-gather.2.cloned.1.call-start = ((), (), s32[]{:S(2)}) async-start(), calls=%async_computation.8 | async-start | bytes 1327104 | tf_op jit(solution)/shard_map/all_gather | solution.py:72
  248.7 1.5 copy-start.6
  472.5 5.0 copy-start.2
  472.5 5.0 copy-start.7
  477.6 2.8 copy-start.4
  578.5 16.8 %copy-start.12 = (bf16[48,8]{0,1:T(8,128)(2,1)S(1)}, bf16[48,8]{0,1:T(8,128)(2,1)}, u32[]{:S(2)}) copy-start(bf16[48,8]{0,1:T(8,128)(2,1)} %param.12) | copy-start | bytes 2308
  579.7 46.5 %all-to-all-start.7 = ((bf16[64,12,512]{2,1,0:T(8,128)(2,1)}), bf16[64,12,512]{2,1,0:T(8,128)(2,1)S(1)}, u32[]{:S(2)}, u32[]{:S(2)}) async-start(bf16[64,12,512]{2,1,0:T(8,128)(2,1)} %reshape.113), calls=%async_computation.7 | async-start | bytes 2097152 | tf_op jit(solution)/shard_map/all_to_all | solution.py:79
  598.8 28.4 %copy-start.1 = (s32[64]{0:T(128)S(1)}, s32[64]{0:T(128)}, u32[]{:S(2)}) copy-start(s32[64]{0:T(128)} %param.14) | copy-start | bytes 772
Sparse Core Ops, SparseCore 0:
  480.5 95.6 all-gather.1
where the time goes:
time: 641 us; the launch traced here: 634 us
  waiting for transfers between devices  333 us (52%)
  blocking collectives  92 us (14%)
  starting transfers between devices  70.7 us (11%)
  local copies, waits for them, and re-layouts  66.9 us (10%)
  other arithmetic  41.2 us (6%)
  matrix products  15.4 us (2%)
  between operations  14.8 us (2%)
    all_to_all x1, waiting for transfers between devices, body(): lax.all_to_all(outgoing.reshape(groups, capacity, -1), 'expert', split_ax...  206 us
    all_to_all x1, blocking collectives, body(): lax.all_to_all(down_order, 'expert', split_axis=0, concat_axis=0, tiled=T...  54.6 us
    all_gather x1, blocking collectives, body(): full_tokens = lax.all_gather(tokens, 'narrow', axis=1, tiled=True)  37.4 us
    all_gather x1, waiting for transfers between devices, body(): lax.all_gather(hidden, 'narrow', axis=1, tiled=True)  29.8 us
    all_to_all x1, waiting for transfers between devices, body(): lax.all_to_all(produced, 'expert', split_axis=0, concat_axis=0, tiled=True)  25.5 us
    unnamed x45, local copies, waits for them, and re-layouts  24.1 us
    all_to_all x1, waiting for transfers between devices, body(): lax.all_to_all(up_order, 'expert', split_axis=0, concat_axis=0, tiled=True)  22.8 us
    all_to_all x1, waiting for transfers between devices, body(): lax.all_to_all(down_flat, 'expert', split_axis=0, concat_axis=0, tiled=True)  17.1 us
  transfers between devices with their start and end apart: 8, of which 7 were waited for; matrix products, arithmetic and copies ran while one was open for 12% of the time, Pallas kernels for 0%

commit v1 on v0

--- a/solution.py
+++ b/solution.py
@@ -56,7 +56,9 @@
     up_block = new_up[0]
     down_block = new_down[0]
     dispatch, combine, capacity = slot_layout(route_ids, route_weight, holder, groups)
-    full_tokens = lax.all_gather(tokens, "narrow", axis=1, tiled=True)
+    full_tokens = jnp.concatenate(
+        lax.all_to_all(jnp.stack([tokens] * lax.axis_size("narrow")), "narrow", 0, 0), axis=1
+    )
     outgoing = jnp.dot(dispatch, full_tokens, preferred_element_type=jnp.float32).astype(
         jnp.bfloat16
     )

time: 641 us -> 604 us (0.942)
  blocking collectives: 92 us -> 45.7 us
  waiting for transfers between devices: 333 us -> 346 us
    all_gather x1 -> x0, blocking collectives: 37.4 us -> none  [body(): full_tokens = lax.all_gather(tokens, 'narrow', axis=1, tiled=True)]
    all_to_all x1, starting transfers between devices: 15.7 us -> 5.74 us  [body(): lax.all_to_all(outgoing.reshape(groups, capacity, -1), 'expert', split_ax...]
    all_to_all x1, blocking collectives: 54.6 us -> 45.7 us  [body(): lax.all_to_all(down_order, 'expert', split_axis=0, concat_axis=0, tiled=T...]
    all_to_all x1, waiting for transfers between devices: 0.01 us -> 7.88 us  [body(): lax.all_to_all(gate_order, 'expert', split_axis=0, concat_axis=0, tiled=T...]
    all_to_all x1, waiting for transfers between devices: 206 us -> 214 us  [body(): lax.all_to_all(outgoing.reshape(groups, capacity, -1), 'expert', split_ax...]
    unnamed x45 -> x49, local copies, waits for them, and re-layouts: 24.1 us -> 24.3 us
  transfers between devices with their start and end apart: 8 -> 9, of which waited for: 7 -> 8; matrix products, arithmetic and copies ran while one was open for 12% -> 14% of each run, Pallas kernels for 0% -> 0%
where the time goes in v1:
time: 604 us; the launch traced here: 597 us
  waiting for transfers between devices  346 us (57%)
  local copies, waits for them, and re-layouts  67.9 us (11%)
  starting transfers between devices  66.6 us (11%)
  blocking collectives  45.7 us (8%)
  other arithmetic  40.6 us (7%)
  matrix products  15.4 us (3%)
  between operations  14.8 us (2%)
    all_to_all x1, waiting for transfers between devices, body(): lax.all_to_all(outgoing.reshape(groups, capacity, -1), 'expert', split_ax...  214 us
    all_to_all x1, blocking collectives, body(): lax.all_to_all(down_order, 'expert', split_axis=0, concat_axis=0, tiled=T...  45.7 us
    all_gather x1, waiting for transfers between devices, body(): lax.all_gather(hidden, 'narrow', axis=1, tiled=True)  26.9 us
    all_to_all x1, waiting for transfers between devices, body(): lax.all_to_all(produced, 'expert', split_axis=0, concat_axis=0, tiled=True)  25.5 us
    unnamed x49, local copies, waits for them, and re-layouts  24.3 us
    all_to_all x1, waiting for transfers between devices, body(): lax.all_to_all(up_order, 'expert', split_axis=0, concat_axis=0, tiled=True)  22.9 us
    all_to_all x1, waiting for transfers between devices, body(): lax.all_to_all(down_flat, 'expert', split_axis=0, concat_axis=0, tiled=True)  17.1 us
    all_to_all x1, waiting for transfers between devices, body(): lax.all_to_all(gate_flat, 'expert', split_axis=0, concat_axis=0, tiled=True)  17 us
  transfers between devices with their start and end apart: 9, of which 8 were waited for; matrix products, arithmetic and copies ran while one was open for 14% of the time, Pallas kernels for 0%

profile of v1, /device:TPU:80, one launch (start us, length us, event | category | flops | bytes accessed | tf_op | source)
XLA Modules:
  0.0 597.1 jit_solution(8275535595310786972)
XLA Ops:
  12.4 5.4 reduce.9
  19.3 16.0 %all-to-all-start.6 = ((bf16[64,2,3072]{2,1,0:T(2,128)(2,1)}), bf16[64,2,3072]{2,1,0:T(2,128)(2,1)S(1)}, u32[]{:S(2)}, u32[]{:S(2)}) async-start(bf16[64,2,3072]{2,1,0:T(2,128)(2,1)} %reshape.185), calls=%async_computation.6 | async-start | bytes 1572864 | tf_op jit(solution)/shard_map/all_to_all | solution.py:41
  36.6 5.4 reduce.10
  43.5 17.1 %all-to-all-done.6 = bf16[64,2,3072]{2,1,0:T(2,128)(2,1)S(1)} async-done(((bf16[64,2,3072]{2,1,0:T(2,128)(2,1)}), bf16[64,2,3072]{2,1,0:T(2,128)(2,1)S(1)}, u32[]{:S(2)}, u32[]{:S(2)}) %all-to-all-start.6) | async-done | bytes 786464 | tf_op jit(solution)/shard_map/all_to_all | solution.py:41
  60.6 6.1 %all-to-all-start.2 = ((bf16[64,2,3072]{2,1,0:T(2,128)(2,1)}), bf16[64,2,3072]{2,1,0:T(2,128)(2,1)}, u32[]{:S(2)}, u32[]{:S(2)}) async-start(bf16[64,2,3072]{2,1,0:T(2,128)(2,1)} %reshape.181), calls=%async_computation.2 | async-start | bytes 1572864 | tf_op jit(solution)/shard_map/all_to_all | solution.py:39
  68.0 5.4 reduce.11
  74.9 17.0 %all-to-all-done.2 = bf16[64,2,3072]{2,1,0:T(2,128)(2,1)} async-done(((bf16[64,2,3072]{2,1,0:T(2,128)(2,1)}), bf16[64,2,3072]{2,1,0:T(2,128)(2,1)}, u32[]{:S(2)}, u32[]{:S(2)}) %all-to-all-start.2) | async-done | bytes 786464 | tf_op jit(solution)/shard_map/all_to_all | solution.py:39
  91.9 5.7 all-to-all-start.4
  107.9 15.2 %all-to-all-done.4 = bf16[64,2,3072]{2,1,0:T(2,128)(2,1)} async-done(((bf16[64,2,3072]{2,1,0:T(2,128)(2,1)}), bf16[64,2,3072]{2,1,0:T(2,128)(2,1)}, u32[]{:S(2)}, u32[]{:S(2)}) %all-to-all-start.4) | async-done | bytes 786464 | tf_op jit(solution)/shard_map/all_to_all | solution.py:40
  123.8 6.2 %all-to-all-start = ((bf16[8,48,512]{2,1,0:T(8,128)(2,1)}), bf16[8,48,512]{2,1,0:T(8,128)(2,1)S(1)}, u32[]{:S(2)}, u32[]{:S(2)}) async-start(bf16[8,48,512]{2,1,0:T(8,128)(2,1)} %stack.2), calls=%async_computation | async-start | bytes 786432 | tf_op jit(solution)/shard_map/all_to_all | solution.py:60
  141.7 5.5 all-to-all-start.5
  149.8 22.9 %all-to-all-done.5 = bf16[64,2,3072]{2,1,0:T(2,128)(2,1)S(1)} async-done(((bf16[64,2,3072]{2,1,0:T(2,128)(2,1)}), bf16[64,2,3072]{2,1,0:T(2,128)(2,1)S(1)}, u32[]{:S(2)}, u32[]{:S(2)}) %all-to-all-start.5) | async-done | bytes 786464 | tf_op jit(solution)/shard_map/all_to_all | solution.py:48
  172.7 5.5 all-to-all-start.3
  186.1 9.7 %reshape.121 = bf16[64,12,4096]{2,1,0:T(8,128)(2,1)} reshape(bf16[768,4096]{1,0:T(8,128)(2,1)} %convolution_convert_fusion) | data formatting | bytes 12582912 | tf_op jit(solution)/shard_map/reshape | solution.py:66
  195.8 7.9 %all-to-all-done.3 = bf16[64,2,3072]{2,1,0:T(2,128)(2,1)S(1)} async-done(((bf16[64,2,3072]{2,1,0:T(2,128)(2,1)}), bf16[64,2,3072]{2,1,0:T(2,128)(2,1)S(1)}, u32[]{:S(2)}, u32[]{:S(2)}) %all-to-all-start.3) | async-done | bytes 786464 | tf_op jit(solution)/shard_map/all_to_all | solution.py:47
  204.6 5.7 all-to-all-start.1
  223.7 213.5 %all-to-all-done.1 = bf16[64,12,4096]{2,1,0:T(8,128)(2,1)} async-done(((bf16[64,12,4096]{2,1,0:T(8,128)(2,1)}), bf16[64,12,4096]{2,1,0:T(8,128)(2,1)}, u32[]{:S(2)}, u32[]{:S(2)}) %all-to-all-start.1) | async-done | bytes 6291488 | tf_op jit(solution)/shard_map/all_to_all | solution.py:65
  437.2 10.0 %reshape.122 = bf16[768,4096]{1,0:T(8,128)(2,1)} reshape(bf16[64,12,4096]{2,1,0:T(8,128)(2,1)} %all-to-all-done.1) | data formatting | bytes 12582912 | tf_op jit(solution)/shard_map/reshape | solution.py:68
  447.3 5.0 fusion.6
  456.8 45.7 %all_to_all.81 = bf16[64,2,3072]{2,1,0:T(2,128)(2,1)S(1)} all-to-all(bf16[64,2,3072]{2,1,0:T(2,128)(2,1)S(1)} %reshape.187), channel_id=1, replica_groups=mesh['expert'=64,'narrow'=8] {'expert'}, dimensions={0} | all-to-all | bytes 1572864 | tf_op jit(solution)/shard_map/all_to_all | solution.py:49
  504.4 5.8 reduce.4
  512.0 26.9 %all-gather.2.cloned.1.call-done = bf16[768,768]{0,1:T(8,128)(2,1)} async-done(((bf16[768,96]{0,1:T(8,128)(2,1)}), bf16[768,768]{0,1:T(8,128)(2,1)}) %all-gather.2.cloned.1.call-update) | async-done | bytes 1179664 | tf_op jit(solution)/shard_map/all_gather | solution.py:74
  542.4 15.6 %all-to-all-start.8 = ((bf16[64,12,512]{2,1,0:T(8,128)(2,1)}), bf16[64,12,512]{2,1,0:T(8,128)(2,1)S(1)}, u32[]{:S(2)}, u32[]{:S(2)}) async-start(bf16[64,12,512]{2,1,0:T(8,128)(2,1)} %reshape.123), calls=%async_computation.8 | async-start | bytes 2097152 | tf_op jit(solution)/shard_map/all_to_all | solution.py:81
  563.4 25.5 %all-to-all-done.8 = bf16[64,12,512]{2,1,0:T(8,128)(2,1)S(1)} async-done(((bf16[64,12,512]{2,1,0:T(8,128)(2,1)}), bf16[64,12,512]{2,1,0:T(8,128)(2,1)S(1)}, u32[]{:S(2)}, u32[]{:S(2)}) %all-to-all-start.8) | async-done | bytes 786464 | tf_op jit(solution)/shard_map/all_to_all | solution.py:81
  (95 shorter events, 77.3 us)
Async XLA Ops:
  7.2 90.5 %copy-start = (s32[64]{0:T(128)S(1)}, s32[64]{0:T(128)}, u32[]{:S(2)}) copy-start(s32[64]{0:T(128)} %param.14) | copy-start | bytes 772
  19.3 16.0 %copy-start.8 = (bf16[1,96,4096]{2,1,0:T(8,128)(2,1)S(1)}, bf16[1,96,4096]{2,1,0:T(8,128)(2,1)}, u32[]{:S(2)}) copy-start(bf16[1,96,4096]{2,1,0:T(8,128)(2,1)} %param.15) | copy-start | bytes 2359300
  19.3 41.3 %all-to-all-start.6 = ((bf16[64,2,3072]{2,1,0:T(2,128)(2,1)}), bf16[64,2,3072]{2,1,0:T(2,128)(2,1)S(1)}, u32[]{:S(2)}, u32[]{:S(2)}) async-start(bf16[64,2,3072]{2,1,0:T(2,128)(2,1)} %reshape.185), calls=%async_computation.6 | async-start | bytes 1572864 | tf_op jit(solution)/shard_map/all_to_all | solution.py:41
  43.5 23.3 %copy-start.9 = (bf16[1,96,4096]{2,1,0:T(8,128)(2,1)S(1)}, bf16[1,96,4096]{2,1,0:T(8,128)(2,1)}, u32[]{:S(2)}) copy-start(bf16[1,96,4096]{2,1,0:T(8,128)(2,1)} %param.16) | copy-start | bytes 2359300
  60.6 31.3 %all-to-all-start.2 = ((bf16[64,2,3072]{2,1,0:T(2,128)(2,1)}), bf16[64,2,3072]{2,1,0:T(2,128)(2,1)}, u32[]{:S(2)}, u32[]{:S(2)}) async-start(bf16[64,2,3072]{2,1,0:T(2,128)(2,1)} %reshape.181), calls=%async_computation.2 | async-start | bytes 1572864 | tf_op jit(solution)/shard_map/all_to_all | solution.py:39
  73.5 24.2 %copy-start.15 = (s32[64]{0:T(128)S(1)}, s32[64]{0:T(128)}, u32[]{:S(2)}) copy-start(s32[64]{0:T(128)} %param.13) | copy-start | bytes 772
  91.9 31.1 %all-to-all-start.4 = ((bf16[64,2,3072]{2,1,0:T(2,128)(2,1)}), bf16[64,2,3072]{2,1,0:T(2,128)(2,1)}, u32[]{:S(2)}, u32[]{:S(2)}) async-start(bf16[64,2,3072]{2,1,0:T(2,128)(2,1)} %reshape.177), calls=%async_computation.4 | async-start | bytes 1572864 | tf_op jit(solution)/shard_map/all_to_all | solution.py:40
  106.0 17.1 %copy-start.12 = (bf16[48,512]{1,0:T(8,128)(2,1)S(1)}, bf16[48,512]{1,0:T(8,128)(2,1)}, u32[]{:S(2)}) copy-start(bf16[48,512]{1,0:T(8,128)(2,1)} %param.10) | copy-start | bytes 147460
  123.8 17.8 %all-to-all-start = ((bf16[8,48,512]{2,1,0:T(8,128)(2,1)}), bf16[8,48,512]{2,1,0:T(8,128)(2,1)S(1)}, u32[]{:S(2)}, u32[]{:S(2)}) async-start(bf16[8,48,512]{2,1,0:T(8,128)(2,1)} %stack.2), calls=%async_computation | async-start | bytes 786432 | tf_op jit(solution)/shard_map/all_to_all | solution.py:60
  135.4 1.1 copy-start.3
  141.7 31.0 %all-to-all-start.5 = ((bf16[64,2,3072]{2,1,0:T(2,128)(2,1)}), bf16[64,2,3072]{2,1,0:T(2,128)(2,1)S(1)}, u32[]{:S(2)}, u32[]{:S(2)}) async-start(bf16[64,2,3072]{2,1,0:T(2,128)(2,1)} %reshape.179), calls=%async_computation.5 | async-start | bytes 1572864 | tf_op jit(solution)/shard_map/all_to_all | solution.py:48
  148.3 29.9 %copy-start.13 = (s32[48,8]{0,1:T(8,128)S(1)}, s32[48,8]{0,1:T(8,128)}, u32[]{:S(2)}) copy-start(s32[48,8]{0,1:T(8,128)} %param.11) | copy-start | bytes 4612
  172.7 31.0 %all-to-all-start.3 = ((bf16[64,2,3072]{2,1,0:T(2,128)(2,1)}), bf16[64,2,3072]{2,1,0:T(2,128)(2,1)S(1)}, u32[]{:S(2)}, u32[]{:S(2)}) async-start(bf16[64,2,3072]{2,1,0:T(2,128)(2,1)} %reshape.183), calls=%async_computation.3 | async-start | bytes 1572864 | tf_op jit(solution)/shard_map/all_to_all | solution.py:47
  203.7 0.9 copy-start.5
  204.6 232.6 %all-to-all-start.1 = ((bf16[64,12,4096]{2,1,0:T(8,128)(2,1)}), bf16[64,12,4096]{2,1,0:T(8,128)(2,1)}, u32[]{:S(2)}, u32[]{:S(2)}) async-start(bf16[64,12,4096]{2,1,0:T(8,128)(2,1)} %reshape.121), calls=%async_computation.1 | async-start | bytes 16777216 | tf_op jit(solution)/shard_map/all_to_all | solution.py:65
  210.3 328.6 %all-gather.2.cloned.1.call-start = ((), (), s32[]{:S(2)}) async-start(), calls=%async_computation.9 | async-start | bytes 1327104 | tf_op jit(solution)/shard_map/all_gather | solution.py:74
  216.1 1.5 copy-start.6
  447.3 5.0 copy-start.2
  447.3 5.0 copy-start.7
  452.3 2.8 copy-start.4
  541.2 16.8 %copy-start.14 = (bf16[48,8]{0,1:T(8,128)(2,1)S(1)}, bf16[48,8]{0,1:T(8,128)(2,1)}, u32[]{:S(2)}) copy-start(bf16[48,8]{0,1:T(8,128)(2,1)} %param.12) | copy-start | bytes 2308
  541.3 16.9 %copy-start.11 = (s32[48,8]{1,0:T(8,128)S(1)}, s32[48,8]{1,0:T(8,128)}, u32[]{:S(2)}) copy-start(s32[48,8]{1,0:T(8,128)} %copy-done.10) | copy-start | bytes 4612
  542.4 46.5 %all-to-all-start.8 = ((bf16[64,12,512]{2,1,0:T(8,128)(2,1)}), bf16[64,12,512]{2,1,0:T(8,128)(2,1)S(1)}, u32[]{:S(2)}, u32[]{:S(2)}) async-start(bf16[64,12,512]{2,1,0:T(8,128)(2,1)} %reshape.123), calls=%async_computation.8 | async-start | bytes 2097152 | tf_op jit(solution)/shard_map/all_to_all | solution.py:81
  561.5 28.4 %copy-start.1 = (s32[64]{0:T(128)S(1)}, s32[64]{0:T(128)}, u32[]{:S(2)}) copy-start(s32[64]{0:T(128)} %param.14) | copy-start | bytes 772
  (1 other events, 0.6 us)
Sparse Core Ops, SparseCore 0:
  455.2 83.6 all-gather.1
